TPU v7x, 256 devices: a whole 4x4x8 slice. The times are simulated.
256 devices in a mesh: req: 8 (over z), exp: 8 (over y, core), hid: 4 (over x).
Axes of the slice: x: 4, y: 4, z: 8, core: 2. Of those that a mesh axis runs over, the one named last changes fastest.
Arguments:
- layer_input_rows: bfloat16 [16384, 1536], P(('req', 'exp')), may hold values from -6 to 6
- attention_norm_gain: float32 [1536], replicated
- query_weight: bfloat16 [1536, 1536], P(None, 'hid'), may hold values from -1 to 1
- key_weight: bfloat16 [1536, 512], P(None, 'hid'), may hold values from -1 to 1
- value_weight: bfloat16 [1536, 512], P(None, 'hid'), may hold values from -0.15625 to 0.15625
- attention_output_weight: bfloat16 [1536, 1536], P('hid'), may hold values from -0.15625 to 0.15625
- query_down_factor: bfloat16 [64, 1536, 16], P(('req', 'exp')), may hold values from -0.15625 to 0.15625
- query_up_factor: bfloat16 [64, 16, 1536], P(('req', 'exp')), may hold values from -1.5 to 1.5
- value_down_factor: bfloat16 [64, 1536, 16], P(('req', 'exp')), may hold values from -0.15625 to 0.15625
- value_up_factor: bfloat16 [64, 16, 512], P(('req', 'exp')), may hold values from -1.5 to 1.5
- lengths: int32 [8, 4], P('req'), may hold values from 1 to 1024, 2048 in all within a row
- request_adapter: int32 [8, 4], replicated, may hold values from 0 to 63
- adapter_home_row: int32 [64], replicated, may hold values from 0 to 63, each once
- expert_norm_gain: float32 [1536], replicated, may hold values from 0.4 to 1.6
- routes: int32 [16384, 8], P(('req', 'exp', 'hid')), may hold values from 0 to 39, all different within a row; in each aligned block of 64 rows (0 to 63, 64 to 127, ...) at most 16 rows name the same one
- router_expert_weight: float32 [16384, 8], P(('req', 'exp', 'hid')), may hold values from 0.1 to 0.5
- expert_gate_weight: bfloat16 [40, 1536, 512], P('exp', None, 'hid'), may hold values from -0.15625 to 0.15625
- expert_up_weight: bfloat16 [40, 1536, 512], P('exp', None, 'hid'), may hold values from -0.15625 to 0.15625
- expert_down_weight: bfloat16 [40, 512, 1536], P('exp', 'hid'), may hold values from -0.25 to 0.25
Outputs:
- attn_out: bfloat16 [16384, 1536], P(('req', 'exp', 'hid'))
- expert_out: bfloat16 [16384, 1536], P(('req', 'exp', 'hid'))
Inputs may be any that keep to these rules, and one draw needn't show every extreme that they name: `lengths`: each row sums to 2048; its largest entry is exactly 1024. `adapter_home_row`: each adapter row appears once. `routes`: A row names 8 different experts. In the rows of one device (64 consecutive rows, aligned) no expert is named more than 16 times, a bound that some block reaches in some of them.
All inputs are finite; a program needn't handle non-finite values.
Results may differ from a plain program's by a relative error of at most 0.029.
The roundings to bfloat16 on the way count: a program that leaves them out, or rounds other values in their place, can miss the bound.
Values may be sent and summed in bfloat16 or wider, within the bound.
No kernel may reach another device: no remote copies, remote signals or barrier semaphores. Data moves between devices by JAX's collectives and lax.ppermute only.
A program may use at most 128 MiB of HBM per device.

v0:
```python
import jax
import jax.numpy as jnp
from jax import lax
from jax.sharding import PartitionSpec as P

HEAD_WIDTH = 64
scale_attn = 0.015625
residual_mult = 0.22
norm_eps = 1e-06
rope_base = 10000.0
neg_large = -1e30


def rms_norm(values, norm_gain):
    widened = values.astype(jnp.float32)
    mean_sq = jnp.mean(widened * widened, axis=-1, keepdims=True)
    return (widened * lax.rsqrt(mean_sq + norm_eps) * norm_gain).astype(jnp.bfloat16)


def rotary(heads_in, position):
    half_size = heads_in.shape[-1] // 2
    frequency = rope_base ** (-2.0 * jnp.arange(half_size, dtype=jnp.float32) / heads_in.shape[-1])
    angles = position.astype(jnp.float32)[:, None] * frequency[None, :]
    cosine = jnp.cos(angles)[:, None, :]
    sine_part = jnp.sin(angles)[:, None, :]
    first_half = heads_in[..., :half_size]
    second_half = heads_in[..., half_size:]
    return jnp.concatenate(
        [
            first_half * cosine - second_half * sine_part,
            second_half * cosine + first_half * sine_part,
        ],
        axis=-1,
    )


def request_of(row_ids, group_len):
    request_end = jnp.cumsum(group_len)
    return jnp.sum((row_ids[:, None] >= request_end[None, :]).astype(jnp.int32), axis=1)


def locate(row_ids, group_len):
    request_end = jnp.cumsum(group_len)
    request_start = request_end - group_len
    request = request_of(row_ids, group_len)
    member = request[:, None] == jnp.arange(group_len.shape[0], dtype=jnp.int32)[None, :]
    position = row_ids - jnp.sum(jnp.where(member, request_start[None, :], 0), axis=1)
    return (request, member, position)


def expert_rows(rows_in, expert_gate_weight, expert_up_weight, expert_down_weight):
    gate_act = jnp.einsum(
        "red,edf->ref", rows_in, expert_gate_weight, preferred_element_type=jnp.float32
    )
    upper = jnp.einsum(
        "red,edf->ref", rows_in, expert_up_weight, preferred_element_type=jnp.float32
    )
    hidden = (jax.nn.silu(gate_act) * upper).astype(jnp.bfloat16)
    return jnp.einsum(
        "ref,efd->red", hidden, expert_down_weight, preferred_element_type=jnp.float32
    )


def per_device(
    layer_input_rows,
    attention_norm_gain,
    query_weight,
    key_weight,
    value_weight,
    attention_output_weight,
    query_down_factor,
    query_up_factor,
    value_down_factor,
    value_up_factor,
    lengths,
    request_adapter,
    adapter_home_row,
    expert_norm_gain,
    routes,
    router_expert_weight,
    expert_gate_weight,
    expert_up_weight,
    expert_down_weight,
):
    exp_count = lax.axis_size("exp")
    hid_count = lax.axis_size("hid")
    exp_index = lax.axis_index("exp")
    hid_index = lax.axis_index("hid")
    req_index = lax.axis_index("req")
    query_rows = layer_input_rows.shape[0]
    width = layer_input_rows.shape[1]
    kv_local = key_weight.shape[1] // HEAD_WIDTH
    q_local = query_weight.shape[1] // HEAD_WIDTH
    group_share = q_local // kv_local
    adapter_rank_size = query_down_factor.shape[2]
    requests = lengths.shape[1]
    group_len = lengths[0]
    row_ids = exp_index * query_rows + jnp.arange(query_rows, dtype=jnp.int32)
    request, member, position = locate(row_ids, group_len)
    wanted = lax.dynamic_index_in_dim(request_adapter, req_index, 0, keepdims=False)
    slot_ids = jnp.arange(adapter_home_row.shape[0], dtype=jnp.int32)
    home_of = jnp.sum(
        jnp.where(wanted[:, None] == slot_ids[None, :], adapter_home_row[None, :], 0), axis=1
    )
    pieces = (
        lax.all_gather(query_down_factor, ("req", "exp"), axis=0, tiled=True),
        lax.all_gather(query_up_factor, ("req", "exp"), axis=0, tiled=True),
        lax.all_gather(value_down_factor, ("req", "exp"), axis=0, tiled=True),
        lax.all_gather(value_up_factor, ("req", "exp"), axis=0, tiled=True),
    )
    adapter_bank_rows = jnp.arange(pieces[0].shape[0], dtype=jnp.int32)
    selector = (home_of[:, None] == adapter_bank_rows[None, :]).astype(jnp.bfloat16)
    picked_now = tuple(
        (
            jnp.einsum("jn,nab->jab", selector, piece_in, preferred_element_type=jnp.float32)
            for piece_in in pieces
        )
    )
    chosen = tuple((fresh for fresh in picked_now))
    qa_sel, qb_sel, va_sel, vb_sel = [member_in.astype(jnp.bfloat16) for member_in in chosen]
    normed_rows = rms_norm(layer_input_rows, attention_norm_gain)

    def low_rank_term(a_sel, b_sel, width_cols, offset):
        inner_terms = jnp.einsum(
            "td,jdr->tjr", normed_rows, a_sel, preferred_element_type=jnp.float32
        )
        inner_terms = (
            jnp.where(member[:, :, None], inner_terms, 0.0)
            .reshape(query_rows, requests * adapter_rank_size)
            .astype(jnp.bfloat16)
        )
        right_factor = lax.dynamic_slice_in_dim(b_sel, offset, width_cols, 2).reshape(
            requests * adapter_rank_size, width_cols
        )
        return jnp.dot(inner_terms, right_factor, preferred_element_type=jnp.float32)

    query_cols = q_local * HEAD_WIDTH
    kv_cols = kv_local * HEAD_WIDTH
    query_matrix = jnp.dot(
        normed_rows, query_weight, preferred_element_type=jnp.float32
    ) + low_rank_term(qa_sel, qb_sel, query_cols, hid_index * query_cols)
    query_matrix = rotary(query_matrix.reshape(query_rows, q_local, HEAD_WIDTH), position).astype(
        jnp.bfloat16
    )
    query_matrix = query_matrix.reshape(query_rows, kv_local, group_share, HEAD_WIDTH)
    keys_own = jnp.dot(normed_rows, key_weight, preferred_element_type=jnp.float32)
    keys_own = (
        rotary(keys_own.reshape(query_rows, kv_local, HEAD_WIDTH), position)
        .astype(jnp.bfloat16)
        .reshape(query_rows, kv_cols)
    )
    values_own = jnp.dot(
        normed_rows, value_weight, preferred_element_type=jnp.float32
    ) + low_rank_term(va_sel, vb_sel, kv_cols, hid_index * kv_cols)
    values_own = values_own.astype(jnp.bfloat16)
    running_max = jnp.full((kv_local, group_share, query_rows), neg_large, jnp.float32)
    key_piece = lax.all_gather(keys_own, "exp", axis=0, tiled=True)
    value_piece = lax.all_gather(values_own, "exp", axis=0, tiled=True)
    piece_len = key_piece.shape[0]
    key_ids = jnp.arange(piece_len, dtype=jnp.int32)
    key_request = request_of(key_ids, group_len)
    allowed = (request[:, None] == key_request[None, :]) & (key_ids[None, :] <= row_ids[:, None])
    key_heads = key_piece.reshape(piece_len, kv_local, HEAD_WIDTH)
    value_heads = value_piece.reshape(piece_len, kv_local, HEAD_WIDTH)
    scores = (
        jnp.einsum("qkgh,nkh->kgqn", query_matrix, key_heads, preferred_element_type=jnp.float32)
        * scale_attn
    )
    scores = jnp.where(allowed[None, None], scores, neg_large)
    new_max = jnp.maximum(running_max, jnp.max(scores, axis=-1))
    weights = jnp.where(allowed[None, None], jnp.exp(scores - new_max[..., None]), 0.0)
    running_sum = jnp.sum(weights, axis=-1)
    running_out = jnp.einsum(
        "kgqn,nkh->kgqh",
        weights.astype(jnp.bfloat16),
        value_heads,
        preferred_element_type=jnp.float32,
    )
    running_max, running_sum, running_out = (new_max, running_sum, running_out)
    attended = (running_out / running_sum[..., None]).astype(jnp.bfloat16)
    attended = jnp.transpose(attended, (2, 0, 1, 3)).reshape(query_rows, query_cols)
    tok_rows = query_rows // hid_count
    attn_out = lax.psum_scatter(
        jnp.dot(attended, attention_output_weight, preferred_element_type=jnp.float32).astype(
            jnp.bfloat16
        ),
        "hid",
        scatter_dimension=0,
        tiled=True,
    )
    own_rows = lax.dynamic_slice_in_dim(layer_input_rows, hid_index * tok_rows, tok_rows, 0)
    mixed_rows = own_rows.astype(jnp.float32) + residual_mult * attn_out.astype(jnp.float32)
    normed_moe = rms_norm(mixed_rows, expert_norm_gain)
    local_exp = expert_gate_weight.shape[0]
    expert_count = local_exp * exp_count
    top_count = routes.shape[1]
    capacity = max(2, tok_rows // 4)
    flat_route = routes.reshape(tok_rows * top_count)
    route_hits = (flat_route[:, None] == jnp.arange(expert_count, dtype=jnp.int32)[None, :]).astype(
        jnp.int32
    )
    earlier = jnp.cumsum(route_hits, axis=0) - route_hits
    slot_pos = jnp.sum(earlier * route_hits, axis=1)
    slots = slot_pos * expert_count + flat_route
    slot_table = jnp.arange(capacity * expert_count, dtype=jnp.int32)
    placed = jnp.any(
        slot_table[:, None, None] == slots.reshape(tok_rows, top_count)[None], axis=2
    ).astype(jnp.bfloat16)
    outgoing = jnp.dot(placed, normed_moe, preferred_element_type=jnp.float32).astype(jnp.bfloat16)
    outgoing = outgoing.reshape(capacity, expert_count, width)
    copies = jnp.broadcast_to(
        outgoing.reshape(capacity, exp_count, 1, local_exp, width),
        (capacity, exp_count, hid_count, local_exp, width),
    )
    copies = copies.reshape(capacity, exp_count * hid_count * local_exp, width)
    arrived = lax.all_to_all(copies, ("exp", "hid"), split_axis=1, concat_axis=0, tiled=True)
    partials = expert_rows(
        arrived, expert_gate_weight, expert_up_weight, expert_down_weight
    ).astype(jnp.bfloat16)
    returned = lax.all_to_all(partials, ("exp", "hid"), split_axis=0, concat_axis=1, tiled=True)
    returned = returned.reshape(capacity, exp_count, hid_count, local_exp, width)
    results = jnp.sum(returned.astype(jnp.float32), axis=2).astype(jnp.bfloat16)
    results = results.reshape(capacity * expert_count, width)
    picked = jnp.take(results, slots, axis=0).reshape(tok_rows, top_count, width)
    expert_out = jnp.sum(
        router_expert_weight[:, :, None] * picked.astype(jnp.float32), axis=1
    ).astype(jnp.bfloat16)
    return (attn_out, expert_out)


def solution(mesh):
    in_specs = (
        P(("req", "exp"), None),
        P(),
        P(None, "hid"),
        P(None, "hid"),
        P(None, "hid"),
        P("hid", None),
        P(("req", "exp"), None, None),
        P(("req", "exp"), None, None),
        P(("req", "exp"), None, None),
        P(("req", "exp"), None, None),
        P("req", None),
        P(),
        P(),
        P(),
        P(("req", "exp", "hid"), None),
        P(("req", "exp", "hid"), None),
        P("exp", None, "hid"),
        P("exp", None, "hid"),
        P("exp", "hid", None),
    )
    out_specs = (P(("req", "exp", "hid"), None), P(("req", "exp", "hid"), None))
    return jax.shard_map(
        per_device, mesh=mesh, in_specs=in_specs, out_specs=out_specs, check_vma=False
    )
```

profile of v0, /device:TPU:1, one launch (start us, length us, event | category | flops | bytes accessed | tf_op | source)
XLA Modules:
  0.0 728.0 jit_solution(7659078790844080535)
XLA Ops:
  15.1 1.7 fusion.82
  17.4 17.2 %all_gather.18 = bf16[2048,128]{0,1:T(8,128)(2,1)} all-gather(bf16[256,128]{0,1:T(8,128)(2,1)S(1)} %bitcast.138), channel_id=1, replica_groups=mesh['req'=8,'exp'=8,'hid'=4] {'exp'}, dimensions={0}, use_global_device_ids=true | all-gather | bytes 589824 | tf_op jit(solution)/shard_map/all_gather | solution.py:157
  35.2 56.6 %all-gather.11.cloned.1.call-done = bf16[64,16,512]{2,1,0:T(8,128)(2,1)} async-done(((bf16[1,16,512]{2,1,0:T(8,128)(2,1)}), bf16[64,16,512]{2,1,0:T(8,128)(2,1)}) %all-gather.11.cloned.1.call-update) | async-done | bytes 1048592 | tf_op jit(solution)/shard_map/all_gather | solution.py:109
  91.8 2.4 fusion.34
  94.2 76.1 %all-gather.5.cloned.1.call-done = bf16[64,1536,16]{1,2,0:T(8,128)(2,1)} async-done(((bf16[1,1536,16]{1,2,0:T(8,128)(2,1)}), bf16[64,1536,16]{1,2,0:T(8,128)(2,1)}) %all-gather.5.cloned.1.call-update) | async-done | bytes 3145744 | tf_op jit(solution)/shard_map/all_gather | solution.py:106
  170.3 5.3 fusion.12
  175.6 72.9 %all-gather.7.cloned.1.call-done = bf16[64,16,1536]{2,1,0:T(8,128)(2,1)} async-done(((bf16[1,16,1536]{2,1,0:T(8,128)(2,1)}), bf16[64,16,1536]{2,1,0:T(8,128)(2,1)}) %all-gather.7.cloned.1.call-update) | async-done | bytes 3145744 | tf_op jit(solution)/shard_map/all_gather | solution.py:107
  248.5 5.4 fusion.8
  256.1 1.9 copy.89
  259.1 7.7 %fusion = (f32[2,3,256]{2,1,0:T(4,128)S(1)}, f32[2,2048,256,3]{2,1,3,0:T(8,128)}) fusion(pred[256,2048]{0,1:T(8,128)(4,1)S(1)} %fusion.18, bf16[2048,2,64,1]{0,2,3,1:T(8,128)(2,1)} %bitcast.136, bf16[256,2,3,32]{0,3,2,1:T(8,128)(2,1)S(1)} %bitcast.144, bf16[256,2,3,32]{0,3,2,1:T(8,128)(2,1)S(1)} %bitcast.143), kind=kOutput, calls=%fused_computation.3 | convolution fusion | flops 412482048 | bytes 13834240 | tf_op jit(solution)/shard_map/qkgh,nkh->kgqn/dot_general | solution.py:166
  267.3 59.3 %all-gather.9.cloned.1.call-done = bf16[64,1536,16]{1,2,0:T(8,128)(2,1)} async-done(((bf16[1,1536,16]{1,2,0:T(8,128)(2,1)}), bf16[64,1536,16]{1,2,0:T(8,128)(2,1)}) %all-gather.9.cloned.1.call-update) | async-done | bytes 3145744 | tf_op jit(solution)/shard_map/all_gather | solution.py:108
  326.6 5.8 fusion.15
  333.6 13.2 %all_gather.23 = bf16[2048,128]{1,0:T(8,128)(2,1)S(1)} all-gather(bf16[256,128]{1,0:T(8,128)(2,1)S(1)} %fusion.33), channel_id=1, replica_groups=mesh['req'=8,'exp'=8,'hid'=4] {'exp'}, dimensions={0}, use_global_device_ids=true | all-gather | bytes 589824 | tf_op jit(solution)/shard_map/all_gather | solution.py:158
  347.0 7.5 %fusion.1 = f32[2,3,256]{2,1,0:T(4,128)S(1)} fusion(f32[2,2048,256,3]{2,1,3,0:T(8,128)} %get-tuple-element.11, f32[2,3,256]{2,1,0:T(4,128)} %broadcast_maximum_fusion, pred[256,2048]{0,1:T(8,128)(4,1)S(1)} %fusion.18), kind=kLoop, calls=%fused_computation.4 | loop fusion | flops 15727104 | bytes 13119488 | tf_op jit(solution)/shard_map/reduce_sum | solution.py:172
  355.3 3.6 fusion.39
  358.9 1.5 convolution_convert_fusion.1
  363.0 17.3 %reduce-scatter.2.cloned.1.call-done = bf16[64,1536]{1,0:T(8,128)(2,1)} async-done(((bf16[256,1536]{1,0:T(8,128)(2,1)}), bf16[64,1536]{1,0:T(8,128)(2,1)}) %reduce-scatter.2.cloned.1.call-update) | async-done | bytes 196624 | tf_op jit(solution)/shard_map/reduce_scatter | solution.py:183
  381.5 3.0 convolution_convert_fusion
  384.4 4.3 broadcast_in_dim.129
  388.7 3.2 copy.103
  392.8 98.3 %all_to_all.33 = bf16[16,160,1536]{2,0,1:T(8,128)(2,1)S(1)} all-to-all(bf16[16,160,1536]{2,0,1:T(8,128)(2,1)S(1)} %bitcast.131), channel_id=1, replica_groups=mesh['req'=8,'exp'=8,'hid'=4] {'exp','hid'}, dimensions={1} | all-to-all | bytes 15728640 | tf_op jit(solution)/shard_map/all_to_all | solution.py:216
  491.1 3.9 copy.104
  495.0 6.0 convolution_bitcast_fusion.1
  501.0 12.2 %convert_bitcast_fusion = bf16[512,5,1536]{2,0,1:T(8,128)(2,1)} fusion(bf16[5,128,1536]{2,1,0:T(8,128)(2,1)S(1)} %copy-done, bf16[512,5,1536]{2,0,1:T(8,128)(2,1)} %bitcast.134, bf16[5,1536,128]{2,1,0:T(8,128)(2,1)} %param.36, f32[512,5,128]{2,0,1:T(8,128)S(1)} %convolution_bitcast_fusion.1), kind=kOutput, calls=%fused_computation.6 | convolution fusion | flops 2019164160 | bytes 20971520 | tf_op jit(solution)/shard_map/ref,efd->red/dot_general | solution.py:59
  513.2 12.0 %copy.105 = bf16[512,5,1536]{2,1,0:T(8,128)(2,1)} copy(bf16[512,5,1536]{2,0,1:T(8,128)(2,1)} %convert_bitcast_fusion) | data formatting | bytes 15728640 | tf_op jit(solution)/shard_map/convert_element_type | solution.py:219
  525.1 5.6 all-to-all-start.1
  531.6 162.9 %all-to-all-done.1 = bf16[512,5,1536]{2,1,0:T(8,128)(2,1)} async-done(((bf16[512,5,1536]{2,1,0:T(8,128)(2,1)}), bf16[512,5,1536]{2,1,0:T(8,128)(2,1)}, u32[]{:S(2)}, u32[]{:S(2)}) %all-to-all-start.1) | async-done | bytes 7864352 | tf_op jit(solution)/shard_map/all_to_all | solution.py:220
  694.5 10.2 %reduce.1 = bf16[16,8,5,1536]{3,2,0,1:T(8,128)(2,1)} reduce(bf16[16,8,4,5,1536]{4,3,0,2,1:T(8,128)(2,1)} %bitcast.39, bf16[]{:T(256)} %constant.89.clone.1), dimensions={2}, to_apply=%region_14.15 | reduce | flops 2949120 | bytes 9830402 | tf_op jit(solution)/shard_map/reduce_sum | solution.py:222
  704.7 3.9 copy.107
  708.6 4.3 reshape.289
  712.9 5.5 gather_fusion
  718.4 2.8 multiply_reduce_fusion
  (105 shorter events, 20.4 us)
Async XLA Ops:
  7.2 493.8 %copy-start = (bf16[5,128,1536]{2,1,0:T(8,128)(2,1)S(1)}, bf16[5,128,1536]{2,1,0:T(8,128)(2,1)}, u32[]{:S(2)}) copy-start(bf16[5,128,1536]{2,1,0:T(8,128)(2,1)} %param.37) | copy-start | bytes 5898244
  7.2 84.6 %all-gather.11.cloned.1.call-start = ((), (), s32[]{:S(2)}) async-start(), calls=%async_computation.6 | async-start | bytes 1064960 | tf_op jit(solution)/shard_map/all_gather | solution.py:109
  7.9 162.4 %all-gather.5.cloned.1.call-start = ((), (), s32[]{:S(2)}) async-start(), calls=%async_computation.3 | async-start | bytes 3194880 | tf_op jit(solution)/shard_map/all_gather | solution.py:106
  8.7 239.9 %all-gather.7.cloned.1.call-start = ((), (), s32[]{:S(2)}) async-start(), calls=%async_computation.4 | async-start | bytes 3194880 | tf_op jit(solution)/shard_map/all_gather | solution.py:107
  9.4 317.2 %all-gather.9.cloned.1.call-start = ((), (), s32[]{:S(2)}) async-start(), calls=%async_computation.5 | async-start | bytes 3194880 | tf_op jit(solution)/shard_map/all_gather | solution.py:108
  10.0 370.3 %reduce-scatter.2.cloned.1.call-start = ((), (), s32[]{:S(2)}) async-start(), calls=%async_computation.7 | async-start | bytes 983040 | tf_op jit(solution)/shard_map/reduce_scatter | solution.py:183
  12.7 157.6 %copy-start.9 = (s32[4]{0:T(128)}, s32[4]{0:T(128)S(1)}, u32[]{:S(2)}) copy-start(s32[4]{0:T(128)S(1)} %select_reduce_fusion.1) | copy-start | bytes 52
  14.9 20.3 %copy-start.14 = (f32[256]{0:T(256)}, f32[256]{0:T(256)S(1)}, u32[]{:S(2)}) copy-start(f32[256]{0:T(256)S(1)} %add_rsqrt_fusion) | copy-start | bytes 3076
  175.6 78.3 %copy-start.3 = (bf16[256,1536]{1,0:T(8,128)(2,1)S(1)}, bf16[256,1536]{1,0:T(8,128)(2,1)}, u32[]{:S(2)}) copy-start(bf16[256,1536]{1,0:T(8,128)(2,1)} %param.19) | copy-start | bytes 2359300
  248.5 5.4 copy-start.15
  248.5 5.5 copy-start.19
  248.5 5.9 copy-start.11
  248.5 6.1 copy-start.17
  259.0 67.5 %copy-start.10 = (s32[4]{0:T(128)S(1)}, s32[4]{0:T(128)}, u32[]{:S(2)}) copy-start(s32[4]{0:T(128)} %copy-done.9) | copy-start | bytes 52
  266.7 65.7 %copy-start.16 = (f32[256]{0:T(256)S(1)}, f32[256]{0:T(256)}, u32[]{:S(2)}) copy-start(f32[256]{0:T(256)} %copy-done.14) | copy-start | bytes 3076
  266.7 65.7 %copy-start.20 = (f32[1536]{0:T(1024)S(1)}, f32[1536]{0:T(1024)}, u32[]{:S(2)}) copy-start(f32[1536]{0:T(1024)} %param.20) | copy-start | bytes 18436
  267.3 65.6 %copy-start.12 = (pred[256,4]{0,1:T(4,128)(4,1)S(1)}, pred[256,4]{0,1:T(4,128)(4,1)}, u32[]{:S(2)}) copy-start(pred[256,4]{0,1:T(4,128)(4,1)} %iota_compare_fusion.5) | copy-start | bytes 3076
  326.6 6.5 copy-start.18
  347.0 8.2 %copy-start.2 = (f32[2,2048,256,3]{2,1,3,0:T(8,128)S(1)}, f32[2,2048,256,3]{2,1,3,0:T(8,128)}, u32[]{:S(2)}) copy-start(f32[2,2048,256,3]{2,1,3,0:T(8,128)} %get-tuple-element.11) | copy-start | bytes 37748740
  347.0 8.2 %copy-start.6 = (f32[2,3,256]{2,1,0:T(4,128)S(1)}, f32[2,3,256]{2,1,0:T(4,128)}, u32[]{:S(2)}) copy-start(f32[2,3,256]{2,1,0:T(4,128)} %broadcast_maximum_fusion) | copy-start | bytes 18436
  355.2 3.6 copy-start.5
  358.9 1.5 copy-start.7
  358.9 21.5 %copy-start.4 = (bf16[256,1536]{1,0:T(8,128)(2,1)S(1)}, bf16[256,1536]{1,0:T(8,128)(2,1)}, u32[]{:S(2)}) copy-start(bf16[256,1536]{1,0:T(8,128)(2,1)} %param.19) | copy-start | bytes 2359300
  358.9 22.6 %copy-start.8 = (f32[1536]{0:T(1024)S(1)}, f32[1536]{0:T(1024)}, u32[]{:S(2)}) copy-start(f32[1536]{0:T(1024)} %param.32) | copy-start | bytes 18436
  525.1 5.8 copy-start.13
  525.1 169.4 %all-to-all-start.1 = ((bf16[512,5,1536]{2,1,0:T(8,128)(2,1)}), bf16[512,5,1536]{2,1,0:T(8,128)(2,1)}, u32[]{:S(2)}, u32[]{:S(2)}) async-start(bf16[512,5,1536]{2,1,0:T(8,128)(2,1)} %copy.105), calls=%async_computation.2 | async-start | bytes 25165824 | tf_op jit(solution)/shard_map/all_to_all | solution.py:220
  712.9 8.3 %copy-start.1 = (bf16[5,128,1536]{2,1,0:T(8,128)(2,1)S(1)}, bf16[5,128,1536]{2,1,0:T(8,128)(2,1)}, u32[]{:S(2)}) copy-start(bf16[5,128,1536]{2,1,0:T(8,128)(2,1)} %param.37) | copy-start | bytes 5898244
Sparse Core Ops, SparseCore 0:
  10.8 80.9 all-gather.10
  94.6 75.7 all-gather.4
  173.1 75.4 all-gather.6
  251.1 75.4 all-gather.8
  360.5 19.7 reduce-scatter.1
where the time goes:
time: 739 us; the launch traced here: 728 us
  waiting for transfers between devices  448 us (61%)
  blocking collectives  129 us (17%)
  matrix products  57.6 us (8%)
  local copies, waits for them, and re-layouts  43.5 us (6%)
  other arithmetic  30.3 us (4%)
  between operations  14.4 us (2%)
    all_to_all x1, waiting for transfers between devices, per_device(): lax.all_to_all(partials, ('exp', 'hid'), split_axis=0, concat_axis=1, til...  163 us
    all_to_all x1, blocking collectives, per_device(): lax.all_to_all(copies, ('exp', 'hid'), split_axis=1, concat_axis=0, tiled...  98.3 us
    all_gather x1, waiting for transfers between devices, per_device(): lax.all_gather(query_down_factor, ('req', 'exp'), axis=0, tiled=True)  76.1 us
    all_gather x1, waiting for transfers between devices, per_device(): lax.all_gather(query_up_factor, ('req', 'exp'), axis=0, tiled=True)  72.9 us
    all_gather x1, waiting for transfers between devices, per_device(): lax.all_gather(value_down_factor, ('req', 'exp'), axis=0, tiled=True)  59.3 us
    all_gather x1, waiting for transfers between devices, per_device(): lax.all_gather(value_up_factor, ('req', 'exp'), axis=0, tiled=True)  56.6 us
    dot_general x4, matrix products, per_device(): jnp.einsum('jn,nab->jab', selector, piece_in, preferred_element_type=jnp....  18.9 us
    reduce_scatter x1, waiting for transfers between devices, per_device(): lax.psum_scatter(jnp.dot(attended, attention_output_weight, preferred_ele...  17.3 us
  transfers between devices with their start and end apart: 6, of which 6 were waited for; matrix products, arithmetic and copies ran while one was open for 5% of the time, Pallas kernels for 0%

commit v1 on v0

--- a/solution.py
+++ b/solution.py
@@ -1,3 +1,4 @@
+import functools
 import jax
 import jax.numpy as jnp
 from jax import lax
@@ -9,6 +10,27 @@
 norm_eps = 1e-06
 rope_base = 10000.0
 neg_large = -1e30
+
+
+def clear_columns(arr_in, dev_axis):
+    dev_count = lax.axis_size(dev_axis)
+    trail = [(ii, (ii + 1) % dev_count) for ii in range(dev_count)]
+    tray = [(ii, (ii - 1) % dev_count) for ii in range(dev_count)]
+    high, part_next = ([arr_in], [arr_in])
+    for _ in range(dev_count // 2):
+        high.append(lax.ppermute(high[-1], axis_name=dev_axis, perm=trail))
+    tick = 0
+    while tick < (dev_count - 1) // 2:
+        part_next.append(lax.ppermute(part_next[-1], perm=tray, axis_name=dev_axis))
+        tick = tick + 1
+    return jnp.roll(
+        jnp.concatenate([*high[::-1], *part_next[1:]], axis=0),
+        (lax.axis_index(dev_axis) - dev_count // 2) * arr_in.shape[0],
+        axis=0,
+    )
+
+
+search_the_meshes = functools.partial(clear_columns, dev_axis="exp")
 
 
 def rms_norm(values, norm_gain):
@@ -154,7 +176,7 @@
     ) + low_rank_term(va_sel, vb_sel, kv_cols, hid_index * kv_cols)
     values_own = values_own.astype(jnp.bfloat16)
     running_max = jnp.full((kv_local, group_share, query_rows), neg_large, jnp.float32)
-    key_piece = lax.all_gather(keys_own, "exp", axis=0, tiled=True)
+    key_piece = search_the_meshes(keys_own)
     value_piece = lax.all_gather(values_own, "exp", axis=0, tiled=True)
     piece_len = key_piece.shape[0]
     key_ids = jnp.arange(piece_len, dtype=jnp.int32)

time: 739 us -> 738 us (level)
  blocking collectives: 129 us -> 112 us
  starting transfers between devices: 5.79 us -> 19.5 us
    all_gather x1 -> x0, blocking collectives: 17.2 us -> none  [per_device(): key_piece = lax.all_gather(keys_own, 'exp', axis=0, tiled=True)]
    ppermute x0 -> x7, starting transfers between devices: none -> 13.7 us  [the longest x3 7.47 us: clear_columns(): part_next.append(lax.ppermute(part_next[-1], perm=tray, axis_name=dev_axis))]
  transfers between devices with their start and end apart: 6 -> 13, of which waited for: 6 -> 11; matrix products, arithmetic and copies ran while one was open for 5% -> 5% of each run, Pallas kernels for 0% -> 0%
where the time goes in v1:
time: 738 us; the launch traced here: 728 us
  waiting for transfers between devices  451 us (61%)
  blocking collectives  112 us (15%)
  matrix products  57.6 us (8%)
  local copies, waits for them, and re-layouts  43.6 us (6%)
  other arithmetic  29.7 us (4%)
  starting transfers between devices  19.5 us (3%)
  between operations  14.5 us (2%)
    all_to_all x1, waiting for transfers between devices, per_device(): lax.all_to_all(partials, ('exp', 'hid'), split_axis=0, concat_axis=1, til...  163 us
    all_to_all x1, blocking collectives, per_device(): lax.all_to_all(copies, ('exp', 'hid'), split_axis=1, concat_axis=0, tiled...  98.3 us
    all_gather x1, waiting for transfers between devices, per_device(): lax.all_gather(query_down_factor, ('req', 'exp'), axis=0, tiled=True)  76.1 us
    all_gather x1, waiting for transfers between devices, per_device(): lax.all_gather(query_up_factor, ('req', 'exp'), axis=0, tiled=True)  72.9 us
    all_gather x1, waiting for transfers between devices, per_device(): lax.all_gather(value_down_factor, ('req', 'exp'), axis=0, tiled=True)  59.3 us
    all_gather x1, waiting for transfers between devices, per_device(): lax.all_gather(value_up_factor, ('req', 'exp'), axis=0, tiled=True)  56.2 us
    dot_general x4, matrix products, per_device(): jnp.einsum('jn,nab->jab', selector, piece_in, preferred_element_type=jnp....  18.9 us
    reduce_scatter x1, waiting for transfers between devices, per_device(): lax.psum_scatter(jnp.dot(attended, attention_output_weight, preferred_ele...  17.3 us
  transfers between devices with their start and end apart: 13, of which 11 were waited for; matrix products, arithmetic and copies ran while one was open for 5% of the time, Pallas kernels for 0%

profile of v1, /device:TPU:1, one launch (start us, length us, event | category | flops | bytes accessed | tf_op | source)
XLA Modules:
  0.0 727.9 jit_solution(2913210809359474492)
XLA Ops:
  15.1 2.7 collective-permute-start
  19.1 2.4 collective-permute-start.1
  25.9 3.0 collective-permute-start.5
  29.8 4.0 collective-permute-start.6
  35.6 56.2 %all-gather.11.cloned.1.call-done = bf16[64,16,512]{2,1,0:T(8,128)(2,1)} async-done(((bf16[1,16,512]{2,1,0:T(8,128)(2,1)}), bf16[64,16,512]{2,1,0:T(8,128)(2,1)}) %all-gather.11.cloned.1.call-update) | async-done | bytes 1048592 | tf_op jit(solution)/shard_map/all_gather | solution.py:131
  91.8 2.4 fusion.34
  94.3 76.1 %all-gather.5.cloned.1.call-done = bf16[64,1536,16]{1,2,0:T(8,128)(2,1)} async-done(((bf16[1,1536,16]{1,2,0:T(8,128)(2,1)}), bf16[64,1536,16]{1,2,0:T(8,128)(2,1)}) %all-gather.5.cloned.1.call-update) | async-done | bytes 3145744 | tf_op jit(solution)/shard_map/all_gather | solution.py:128
  170.3 5.3 fusion.12
  175.7 72.9 %all-gather.7.cloned.1.call-done = bf16[64,16,1536]{2,1,0:T(8,128)(2,1)} async-done(((bf16[1,16,1536]{2,1,0:T(8,128)(2,1)}), bf16[64,16,1536]{2,1,0:T(8,128)(2,1)}) %all-gather.7.cloned.1.call-update) | async-done | bytes 3145744 | tf_op jit(solution)/shard_map/all_gather | solution.py:129
  248.5 5.4 fusion.8
  259.1 7.7 %fusion = (f32[2,3,256]{2,1,0:T(4,128)S(1)}, f32[2,2048,256,3]{2,1,3,0:T(8,128)}) fusion(pred[256,2048]{0,1:T(8,128)(4,1)S(1)} %fusion.18, bf16[2048,2,64,1]{0,2,3,1:T(8,128)(2,1)} %bitcast.141, bf16[256,2,3,32]{0,3,2,1:T(8,128)(2,1)S(1)} %bitcast.147, bf16[256,2,3,32]{0,3,2,1:T(8,128)(2,1)S(1)} %bitcast.146), kind=kOutput, calls=%fused_computation.3 | convolution fusion | flops 412482048 | bytes 13834240 | tf_op jit(solution)/shard_map/qkgh,nkh->kgqn/dot_general | solution.py:188
  267.3 59.3 %all-gather.9.cloned.1.call-done = bf16[64,1536,16]{1,2,0:T(8,128)(2,1)} async-done(((bf16[1,1536,16]{1,2,0:T(8,128)(2,1)}), bf16[64,1536,16]{1,2,0:T(8,128)(2,1)}) %all-gather.9.cloned.1.call-update) | async-done | bytes 3145744 | tf_op jit(solution)/shard_map/all_gather | solution.py:130
  326.6 5.8 fusion.15
  333.6 13.2 %all_gather.19 = bf16[2048,128]{1,0:T(8,128)(2,1)S(1)} all-gather(bf16[256,128]{1,0:T(8,128)(2,1)S(1)} %fusion.33), channel_id=1, replica_groups=mesh['req'=8,'exp'=8,'hid'=4] {'exp'}, dimensions={0}, use_global_device_ids=true | all-gather | bytes 589824 | tf_op jit(solution)/shard_map/all_gather | solution.py:180
  347.0 7.5 %fusion.1 = f32[2,3,256]{2,1,0:T(4,128)S(1)} fusion(f32[2,2048,256,3]{2,1,3,0:T(8,128)} %get-tuple-element.11, f32[2,3,256]{2,1,0:T(4,128)} %broadcast_maximum_fusion, pred[256,2048]{0,1:T(8,128)(4,1)S(1)} %fusion.18), kind=kLoop, calls=%fused_computation.4 | loop fusion | flops 15727104 | bytes 13119488 | tf_op jit(solution)/shard_map/reduce_sum | solution.py:194
  355.3 3.6 fusion.39
  363.0 17.3 %reduce-scatter.2.cloned.1.call-done = bf16[64,1536]{1,0:T(8,128)(2,1)} async-done(((bf16[256,1536]{1,0:T(8,128)(2,1)}), bf16[64,1536]{1,0:T(8,128)(2,1)}) %reduce-scatter.2.cloned.1.call-update) | async-done | bytes 196624 | tf_op jit(solution)/shard_map/reduce_scatter | solution.py:205
  381.5 3.0 convolution_convert_fusion
  384.4 4.3 broadcast_in_dim.129
  388.7 3.2 copy.103
  392.9 98.3 %all_to_all.33 = bf16[16,160,1536]{2,0,1:T(8,128)(2,1)S(1)} all-to-all(bf16[16,160,1536]{2,0,1:T(8,128)(2,1)S(1)} %bitcast.131), channel_id=1, replica_groups=mesh['req'=8,'exp'=8,'hid'=4] {'exp','hid'}, dimensions={1} | all-to-all | bytes 15728640 | tf_op jit(solution)/shard_map/all_to_all | solution.py:238
  491.2 3.9 copy.104
  495.0 6.0 convolution_bitcast_fusion.1
  501.0 12.2 %convert_bitcast_fusion = bf16[512,5,1536]{2,0,1:T(8,128)(2,1)} fusion(bf16[5,128,1536]{2,1,0:T(8,128)(2,1)S(1)} %copy-done, bf16[512,5,1536]{2,0,1:T(8,128)(2,1)} %bitcast.134, bf16[5,1536,128]{2,1,0:T(8,128)(2,1)} %param.36, f32[512,5,128]{2,0,1:T(8,128)S(1)} %convolution_bitcast_fusion.1), kind=kOutput, calls=%fused_computation.6 | convolution fusion | flops 2019164160 | bytes 20971520 | tf_op jit(solution)/shard_map/ref,efd->red/dot_general | solution.py:81
  513.2 12.0 %copy.105 = bf16[512,5,1536]{2,1,0:T(8,128)(2,1)} copy(bf16[512,5,1536]{2,0,1:T(8,128)(2,1)} %convert_bitcast_fusion) | data formatting | bytes 15728640 | tf_op jit(solution)/shard_map/convert_element_type | solution.py:241
  525.1 5.6 all-to-all-start.1
  531.7 162.9 %all-to-all-done.1 = bf16[512,5,1536]{2,1,0:T(8,128)(2,1)} async-done(((bf16[512,5,1536]{2,1,0:T(8,128)(2,1)}), bf16[512,5,1536]{2,1,0:T(8,128)(2,1)}, u32[]{:S(2)}, u32[]{:S(2)}) %all-to-all-start.1) | async-done | bytes 7864352 | tf_op jit(solution)/shard_map/all_to_all | solution.py:242
  694.5 10.2 %reduce.1 = bf16[16,8,5,1536]{3,2,0,1:T(8,128)(2,1)} reduce(bf16[16,8,4,5,1536]{4,3,0,2,1:T(8,128)(2,1)} %bitcast.39, bf16[]{:T(256)} %constant.113.clone.1), dimensions={2}, to_apply=%region_14.15 | reduce | flops 2949120 | bytes 9830402 | tf_op jit(solution)/shard_map/reduce_sum | solution.py:244
  704.7 3.9 copy.107
  708.6 4.3 reshape.289
  712.9 5.4 gather_fusion
  718.3 2.8 multiply_reduce_fusion
  (137 shorter events, 31.0 us)
Async XLA Ops:
  7.2 493.8 %copy-start = (bf16[5,128,1536]{2,1,0:T(8,128)(2,1)S(1)}, bf16[5,128,1536]{2,1,0:T(8,128)(2,1)}, u32[]{:S(2)}) copy-start(bf16[5,128,1536]{2,1,0:T(8,128)(2,1)} %param.37) | copy-start | bytes 5898244
  7.2 18.5 %copy-start.13 = (s32[8,4]{0,1:T(4,128)S(1)}, s32[8,4]{0,1:T(4,128)}, u32[]{:S(2)}) copy-start(s32[8,4]{0,1:T(4,128)} %param.30) | copy-start | bytes 388
  7.2 21.7 %copy-start.21 = (s32[64]{0:T(128)S(1)}, s32[64]{0:T(128)}, u32[]{:S(2)}) copy-start(s32[64]{0:T(128)} %param.31) | copy-start | bytes 772
  7.2 84.6 %all-gather.11.cloned.1.call-start = ((), (), s32[]{:S(2)}) async-start(), calls=%async_computation.6 | async-start | bytes 1064960 | tf_op jit(solution)/shard_map/all_gather | solution.py:131
  7.9 162.4 %all-gather.5.cloned.1.call-start = ((), (), s32[]{:S(2)}) async-start(), calls=%async_computation.3 | async-start | bytes 3194880 | tf_op jit(solution)/shard_map/all_gather | solution.py:128
  8.7 239.9 %all-gather.7.cloned.1.call-start = ((), (), s32[]{:S(2)}) async-start(), calls=%async_computation.4 | async-start | bytes 3194880 | tf_op jit(solution)/shard_map/all_gather | solution.py:129
  9.4 317.2 %all-gather.9.cloned.1.call-start = ((), (), s32[]{:S(2)}) async-start(), calls=%async_computation.5 | async-start | bytes 3194880 | tf_op jit(solution)/shard_map/all_gather | solution.py:130
  10.0 370.3 %reduce-scatter.2.cloned.1.call-start = ((), (), s32[]{:S(2)}) async-start(), calls=%async_computation.7 | async-start | bytes 983040 | tf_op jit(solution)/shard_map/reduce_scatter | solution.py:205
  13.1 8.9 %copy-start.14 = (f32[256]{0:T(256)}, f32[256]{0:T(256)S(1)}, u32[]{:S(2)}) copy-start(f32[256]{0:T(256)S(1)} %add_rsqrt_fusion) | copy-start | bytes 3076
  15.1 4.0 collective-permute-start
  17.8 8.1 %collective-permute-start.4 = (bf16[256,128]{0,1:T(8,128)(2,1)S(1)}, bf16[256,128]{0,1:T(8,128)(2,1)S(1)}, u32[]{:S(2)}, u32[]{:S(2)}) collective-permute-start(bf16[256,128]{0,1:T(8,128)(2,1)S(1)} %bitcast.137), channel_id=1, source_target_pairs={{0,28},{4,0},{8,4},{12,8},{16,12},{20,16},{24,20},{28,24},{1,29},{... | collective-permute-start | bytes 196616 | tf_op jit(solution)/shard_map/ppermute | solution.py:24
  19.1 4.8 collective-permute-start.1
  24.0 4.9 collective-permute-start.2
  25.9 3.9 collective-permute-start.5
  28.9 4.9 collective-permute-start.3
  29.1 141.3 %copy-start.8 = (s32[4]{0:T(128)}, s32[4]{0:T(128)S(1)}, u32[]{:S(2)}) copy-start(s32[4]{0:T(128)S(1)} %select_reduce_fusion.1) | copy-start | bytes 52
  29.8 4.9 collective-permute-start.6
  175.6 78.3 %copy-start.2 = (bf16[256,1536]{1,0:T(8,128)(2,1)S(1)}, bf16[256,1536]{1,0:T(8,128)(2,1)}, u32[]{:S(2)}) copy-start(bf16[256,1536]{1,0:T(8,128)(2,1)} %param.19) | copy-start | bytes 2359300
  248.5 5.5 copy-start.19
  248.5 5.9 copy-start.10
  248.5 6.1 copy-start.17
  259.1 67.5 %copy-start.9 = (s32[4]{0:T(128)S(1)}, s32[4]{0:T(128)}, u32[]{:S(2)}) copy-start(s32[4]{0:T(128)} %copy-done.8) | copy-start | bytes 52
  266.7 65.7 %copy-start.16 = (f32[256]{0:T(256)S(1)}, f32[256]{0:T(256)}, u32[]{:S(2)}) copy-start(f32[256]{0:T(256)} %copy-done.14) | copy-start | bytes 3076
  266.7 65.7 %copy-start.20 = (f32[1536]{0:T(1024)S(1)}, f32[1536]{0:T(1024)}, u32[]{:S(2)}) copy-start(f32[1536]{0:T(1024)} %param.20) | copy-start | bytes 18436
  267.3 65.6 %copy-start.11 = (pred[256,4]{0,1:T(4,128)(4,1)S(1)}, pred[256,4]{0,1:T(4,128)(4,1)}, u32[]{:S(2)}) copy-start(pred[256,4]{0,1:T(4,128)(4,1)} %iota_compare_fusion.5) | copy-start | bytes 3076
  326.6 6.5 copy-start.18
  347.0 8.2 %copy-start.1 = (f32[2,2048,256,3]{2,1,3,0:T(8,128)S(1)}, f32[2,2048,256,3]{2,1,3,0:T(8,128)}, u32[]{:S(2)}) copy-start(f32[2,2048,256,3]{2,1,3,0:T(8,128)} %get-tuple-element.11) | copy-start | bytes 37748740
  347.0 8.2 %copy-start.5 = (f32[2,3,256]{2,1,0:T(4,128)S(1)}, f32[2,3,256]{2,1,0:T(4,128)}, u32[]{:S(2)}) copy-start(f32[2,3,256]{2,1,0:T(4,128)} %broadcast_maximum_fusion) | copy-start | bytes 18436
  358.9 21.5 %copy-start.3 = (bf16[256,1536]{1,0:T(8,128)(2,1)S(1)}, bf16[256,1536]{1,0:T(8,128)(2,1)}, u32[]{:S(2)}) copy-start(bf16[256,1536]{1,0:T(8,128)(2,1)} %param.19) | copy-start | bytes 2359300
  358.9 22.6 %copy-start.7 = (f32[1536]{0:T(1024)S(1)}, f32[1536]{0:T(1024)}, u32[]{:S(2)}) copy-start(f32[1536]{0:T(1024)} %param.32) | copy-start | bytes 18436
  525.1 5.8 copy-start.12
  525.1 169.4 %all-to-all-start.1 = ((bf16[512,5,1536]{2,1,0:T(8,128)(2,1)}), bf16[512,5,1536]{2,1,0:T(8,128)(2,1)}, u32[]{:S(2)}, u32[]{:S(2)}) async-start(bf16[512,5,1536]{2,1,0:T(8,128)(2,1)} %copy.105), calls=%async_computation.2 | async-start | bytes 25165824 | tf_op jit(solution)/shard_map/all_to_all | solution.py:242
  (3 other events, 10.6 us)
Sparse Core Ops, SparseCore 0:
  10.8 80.9 all-gather.10
  94.6 75.7 all-gather.4
  173.1 75.4 all-gather.6
  251.2 75.4 all-gather.8
  360.5 19.7 reduce-scatter.1
